TPU v7x, 32 devices: a whole 2x2x4 slice. The times are simulated.
32 devices in a mesh: grp: 8 (over y, x, core), rep: 4 (over z).
Axes of the slice: x: 2, y: 2, z: 4, core: 2. Of those that a mesh axis runs over, the one named last changes fastest.
Arguments:
- features: bfloat16 [4096, 256], P(('grp', 'rep')), may hold values from -0.0625 to 0.0625
- weight: bfloat16 [256, 256], replicated, may hold values from -0.375 to 0.375
- preact: bfloat16 [4096, 256], P(('grp', 'rep')), may hold values from -6 to 6
- grad_out: bfloat16 [4096, 256], P(('grp', 'rep')), may hold values from -1.5 to 1.5
- degree: int32 [4096], P(('grp', 'rep')), may hold values from 1 to 64
- tile_values: bfloat16 [256, 4, 128, 128], P(('grp', 'rep')), may hold values from 0 to 1
- tile_rows: int32 [256, 4], P(('grp', 'rep')), may hold values from -1 to 3, as said below
Outputs:
- input_grad: float32 [4096, 256], P(('grp', 'rep'))
- weight_grad: float32 [256, 256], replicated
Inputs may be any that keep to these rules, and one draw needn't show every extreme that they name: `tile_rows`: each of the 8 rows of one device (aligned blocks) has up to 4 live slots; in every such block some row has all 4 slots live.
All inputs are finite; a program needn't handle non-finite values.
Results may differ from a plain program's by a relative error of at most 0.013.
Values may be sent and summed in bfloat16 or wider, within the bound.
No kernel may reach another device: no remote copies, remote signals or barrier semaphores. Data moves between devices by JAX's collectives and lax.ppermute only.
A program may use at most 128 MiB of HBM per device.

v0:
```python
import jax
import jax.numpy as jnp
from jax import lax
from jax.sharding import PartitionSpec as P


def tile_masks(tile_rows):
    tile_live = tile_rows >= 0
    clipped = jnp.where(tile_live, tile_rows, 0)
    return (tile_live, clipped)


def per_device(features, weight, preact, grad_out, degree, tile_values, tile_rows):
    rows_here = features.shape[0]
    feature_width = features.shape[1]
    tile_edge = tile_values.shape[2]
    slot_count = tile_values.shape[1]
    row_tiles = lax.axis_size("rep") * rows_here // tile_edge
    inverse = lax.rsqrt(degree.astype(jnp.float32))[:, None]
    grad_pre = jnp.where(preact > 0, grad_out, jnp.zeros_like(grad_out))
    tile_live, clipped = tile_masks(tile_rows)
    scaled = (features.astype(jnp.float32) * inverse).astype(jnp.bfloat16)
    gathered = lax.all_gather(scaled, "grp", axis=0, tiled=True)
    columns = gathered.reshape(-1, tile_edge, feature_width)
    target = jnp.where(tile_live, tile_rows, row_tiles)
    partial_value = jnp.zeros((row_tiles + 1, tile_edge, feature_width), jnp.float32)
    for slot in range(slot_count):
        product = jnp.einsum(
            "cij,cjf->cif", tile_values[:, slot], columns, preferred_element_type=jnp.float32
        )
        partial_value = partial_value.at[target[:, slot]].add(product)
    partial_value = partial_value[:row_tiles]
    summed = lax.psum_scatter(
        partial_value.reshape(row_tiles * tile_edge, feature_width).astype(jnp.bfloat16),
        "rep",
        scatter_dimension=0,
        tiled=True,
    ).astype(jnp.float32)
    aggregated = (summed * inverse).astype(jnp.bfloat16)
    weight_local = lax.dot_general(
        aggregated, grad_pre, (((0,), (0,)), ((), ())), preferred_element_type=jnp.float32
    )
    projected = (
        lax.dot_general(
            grad_pre, weight, (((1,), (1,)), ((), ())), preferred_element_type=jnp.float32
        )
        * inverse
    ).astype(jnp.bfloat16)
    block_rows = lax.all_gather(projected, "rep", axis=0, tiled=True)
    blocks = block_rows.reshape(row_tiles, tile_edge, feature_width)
    picked = jnp.take(blocks, clipped, axis=0)
    picked = jnp.where(tile_live[:, :, None, None], picked, jnp.zeros_like(picked))
    result = jnp.einsum("csij,csif->cjf", tile_values, picked, preferred_element_type=jnp.float32)
    input_grad = (
        lax.psum_scatter(
            result.reshape(rows_here * lax.axis_size("grp"), feature_width),
            "grp",
            scatter_dimension=0,
            tiled=True,
        )
        * inverse
    )
    weight_grad = lax.psum(weight_local, ("grp", "rep"))
    return (input_grad, weight_grad)


def solution(mesh):
    return jax.shard_map(
        per_device,
        mesh=mesh,
        in_specs=(
            P(("grp", "rep"), None),
            P(),
            P(("grp", "rep"), None),
            P(("grp", "rep"), None),
            P(("grp", "rep")),
            P(("grp", "rep"), None, None, None),
            P(("grp", "rep"), None),
        ),
        out_specs=(P(("grp", "rep"), None), P()),
        check_vma=False,
    )
```

profile of v0, /device:TPU:0, one launch (start us, length us, event | category | flops | bytes accessed | tf_op | source)
XLA Modules:
  0.0 254.5 jit_solution(7141739193772190387)
XLA Ops:
  7.2 0.0 copy-start
  7.2 0.0 reduce-scatter.3.cloned.1.call-start
  7.2 0.7 broadcast_select_fusion
  7.9 0.7 broadcast_compare_fusion
  8.6 0.7 convert_rsqrt_fusion
  9.3 0.0 copy-done
  9.3 1.1 fusion.5
  10.4 15.6 %all_gather.6 = bf16[512,256]{1,0:T(8,128)(2,1)S(1)} all-gather(bf16[128,256]{1,0:T(8,128)(2,1)S(1)} %fusion.5), channel_id=1, replica_groups=mesh['grp'=8,'rep'=4] {'rep'}, dimensions={0}, use_global_device_ids=true | all-gather | bytes 327680 | tf_op jit(solution)/shard_map/all_gather | solution.py:49
  26.0 0.1 copy.27
  26.1 0.1 reshape.27
  26.2 0.1 copy.25
  26.3 0.7 copy.26
  26.9 0.0 copy-start.1
  26.9 0.7 gather_fusion
  27.6 0.5 copy-done.1
  28.1 0.0 copy-start.4
  28.1 2.4 fusion
  30.5 0.0 reduce-scatter.3.cloned.1.call-update
  30.5 0.0 reduce-scatter.5.cloned.1.call-start
  30.6 0.5 fusion.21
  31.1 37.1 %reduce-scatter.3.cloned.1.call-done = f32[128,256]{1,0:T(8,128)} async-done(((f32[1024,256]{1,0:T(8,128)}), f32[128,256]{1,0:T(8,128)}) %reduce-scatter.3.cloned.1.call-update) | async-done | bytes 131088 | tf_op jit(solution)/shard_map/reduce_scatter | solution.py:55
  68.2 0.0 copy-done.4
  68.3 1.6 multiply_convert_fusion.1
  69.9 9.8 %all_gather.7 = bf16[1024,256]{1,0:T(8,128)(2,1)S(1)} all-gather(bf16[128,256]{1,0:T(8,128)(2,1)S(1)} %get-tuple-element.10), channel_id=1, replica_groups=mesh['grp'=8,'rep'=4] {'grp'}, dimensions={0}, use_global_device_ids=true | all-gather | bytes 589824 | tf_op jit(solution)/shard_map/all_gather | solution.py:23
  79.7 1.4 convolution_bitcast_fusion.3
  81.1 0.3 convolution_bitcast_fusion.2
  81.4 0.3 convolution_bitcast_fusion.1
  81.8 1.3 convolution_bitcast_fusion
  83.1 2.6 %copy.31 = f32[8,128,256]{2,1,0:T(8,128)} copy(f32[8,128,256]{1,2,0:T(8,128)} %convolution_bitcast_fusion.3) | data formatting | bytes 2097152 | tf_op jit(solution)/shard_map/cij,cjf->cif/dot_general | solution.py:28
  85.6 1.4 copy.34
  87.0 0.0 copy-start.6
  87.0 0.3 copy.37
  87.3 0.3 copy.40
  87.7 0.0 copy-start.5
  87.7 0.0 copy-done.6
  87.7 2.5 scatter_fusion
  90.2 0.0 copy-done.5
  90.2 2.5 scatter_fusion.1
  92.7 1.3 scatter_fusion.2
  94.0 0.0 copy-start.2
  94.0 0.0 copy-start.3
  94.0 1.3 scatter_fusion.3
  95.4 0.7 slice.61
  96.1 0.0 reduce-scatter.5.cloned.1.call-update
  96.1 0.0 all-reduce.2.cloned.1.call-start
  96.2 19.8 %reduce-scatter.5.cloned.1.call-done = bf16[128,256]{1,0:T(8,128)(2,1)} async-done(((bf16[512,256]{1,0:T(8,128)(2,1)}), bf16[128,256]{1,0:T(8,128)(2,1)}) %reduce-scatter.5.cloned.1.call-update) | async-done | bytes 65552 | tf_op jit(solution)/shard_map/reduce_scatter | solution.py:33
  115.9 0.0 copy-done.2
  115.9 0.0 copy-done.3
  115.9 1.8 fusion.16
  117.8 0.0 all-reduce.2.cloned.1.call-update
  117.8 128.5 %all-reduce.2.cloned.1.call-done = f32[256,256]{1,0:T(8,128)} async-done(((f32[256,256]{1,0:T(8,128)}), f32[256,256]{1,0:T(8,128)}) %all-reduce.2.cloned.1.call-update) | async-done | bytes 262160 | tf_op jit(solution)/shard_map/psum | solution.py:63
  246.3 1.7 copy.56
  (2 shorter events, 0.1 us)
Async XLA Ops:
  7.2 2.1 copy-start
  7.2 61.1 %reduce-scatter.3.cloned.1.call-start = ((), (), s32[]{:S(2)}) async-start(), calls=%async_computation.2 | async-start | bytes 1179648 | tf_op jit(solution)/shard_map/reduce_scatter | solution.py:55
  26.9 1.2 copy-start.1
  28.1 40.1 %copy-start.4 = (bf16[128,256]{1,0:T(8,128)(2,1)S(1)}, bf16[128,256]{1,0:T(8,128)(2,1)}, u32[]{:S(2)}) copy-start(bf16[128,256]{1,0:T(8,128)(2,1)} %param.7) | copy-start | bytes 196612
  30.5 85.4 %reduce-scatter.5.cloned.1.call-start = ((), (), s32[]{:S(2)}) async-start(), calls=%async_computation.3 | async-start | bytes 327680 | tf_op jit(solution)/shard_map/reduce_scatter | solution.py:33
  87.0 0.8 copy-start.6
  87.7 2.5 %copy-start.5 = (s32[8]{0:T(128)S(1)}, s32[8]{0:T(128)}, u32[]{:S(2)}) copy-start(s32[8]{0:T(128)} %get-tuple-element.4) | copy-start | bytes 100
  94.0 21.9 %copy-start.2 = (bf16[128,256]{1,0:T(8,128)(2,1)S(1)}, bf16[128,256]{1,0:T(8,128)(2,1)}, u32[]{:S(2)}) copy-start(bf16[128,256]{1,0:T(8,128)(2,1)} %param.10) | copy-start | bytes 196612
  94.0 21.9 %copy-start.3 = (bf16[128,256]{1,0:T(8,128)(2,1)S(1)}, bf16[128,256]{1,0:T(8,128)(2,1)}, u32[]{:S(2)}) copy-start(bf16[128,256]{1,0:T(8,128)(2,1)} %param.9) | copy-start | bytes 196612
  96.1 150.1 %all-reduce.2.cloned.1.call-start = ((), (), s32[]{:S(2)}) async-start(), calls=%async_computation.4 | async-start | bytes 524288 | tf_op jit(solution)/shard_map/psum | solution.py:63
Sparse Core Ops, SparseCore 0:
  30.7 37.5 reduce-scatter.2
  96.3 19.6 reduce-scatter.4
  122.9 123.2 all-reduce.1
where the time goes:
time: 255 us; the launch traced here: 254 us
  waiting for transfers between devices  185 us (73%)
  blocking collectives  25.4 us (10%)
  between operations  13.9 us (5%)
  other arithmetic  11.8 us (5%)
  local copies, waits for them, and re-layouts  9.19 us (4%)
  matrix products  8.64 us (3%)
    psum x1, waiting for transfers between devices, per_device(): weight_grad = lax.psum(weight_local, ('grp', 'rep'))  128 us
    reduce_scatter x1, waiting for transfers between devices, per_device(): lax.psum_scatter(result.reshape(rows_here * lax.axis_size('grp'), feature...  37.1 us
    reduce_scatter x1, waiting for transfers between devices, per_device(): lax.psum_scatter(partial_value.reshape(row_tiles * tile_edge, feature_wid...  19.8 us
    all_gather x1, blocking collectives, per_device(): block_rows = lax.all_gather(projected, 'rep', axis=0, tiled=True)  15.6 us
    all_gather x1, blocking collectives, per_device(): gathered = lax.all_gather(scaled, 'grp', axis=0, tiled=True)  9.77 us
    scatter-add x4, other arithmetic, per_device(): partial_value = partial_value.at[target[:, slot]].add(product)  7.56 us
  transfers between devices with their start and end apart: 3, of which 3 were waited for; matrix products, arithmetic and copies ran while one was open for 0% of the time, Pallas kernels for 0%

commit v1 on v0

--- a/solution.py
+++ b/solution.py
@@ -20,7 +20,16 @@
     grad_pre = jnp.where(preact > 0, grad_out, jnp.zeros_like(grad_out))
     tile_live, clipped = tile_masks(tile_rows)
     scaled = (features.astype(jnp.float32) * inverse).astype(jnp.bfloat16)
-    gathered = lax.all_gather(scaled, "grp", axis=0, tiled=True)
+    ways = lax.axis_size("grp")
+    up = [(d, (d + 1) % ways) for d in range(ways)]
+    down = [(d, (d - 1) % ways) for d in range(ways)]
+    earlier, later = ([scaled], [scaled])
+    for _ in range(ways // 2):
+        earlier.append(lax.ppermute(earlier[-1], "grp", up))
+    for _ in range((ways - 1) // 2):
+        later.append(lax.ppermute(later[-1], "grp", down))
+    line = jnp.concatenate([*earlier[::-1], *later[1:]], axis=0)
+    gathered = jnp.roll(line, (lax.axis_index("grp") - ways // 2) * scaled.shape[0], axis=0)
     columns = gathered.reshape(-1, tile_edge, feature_width)
     target = jnp.where(tile_live, tile_rows, row_tiles)
     partial_value = jnp.zeros((row_tiles + 1, tile_edge, feature_width), jnp.float32)

time: 255 us -> 266 us (1.043)
  waiting for transfers between devices: 185 us -> 198 us
  blocking collectives: 25.4 us -> 15.6 us
  starting transfers between devices: 0.12 us -> 8.06 us
    ppermute x0 -> x7, waiting for transfers between devices: none -> 11 us  [the longest x4 10.5 us: per_device(): earlier.append(lax.ppermute(earlier[-1], 'grp', up))]
    all_gather x1 -> x0, blocking collectives: 9.77 us -> none  [per_device(): gathered = lax.all_gather(scaled, 'grp', axis=0, tiled=True)]
    ppermute x0 -> x7, starting transfers between devices: none -> 7.94 us  [the longest x3 7.93 us: per_device(): later.append(lax.ppermute(later[-1], 'grp', down))]
  transfers between devices with their start and end apart: 3 -> 10, of which waited for: 3 -> 8; matrix products, arithmetic and copies ran while one was open for 0% -> 0% of each run, Pallas kernels for 0% -> 0%
where the time goes in v1:
time: 266 us
  waiting for transfers between devices  198 us (74%)
  blocking collectives  15.6 us (6%)
  between operations  14 us (5%)
  other arithmetic  11.9 us (4%)
  local copies, waits for them, and re-layouts  9.33 us (4%)
  matrix products  8.61 us (3%)
  starting transfers between devices  8.06 us (3%)
    psum x1, waiting for transfers between devices, per_device(): weight_grad = lax.psum(weight_local, ('grp', 'rep'))  128 us
    reduce_scatter x1, waiting for transfers between devices, per_device(): lax.psum_scatter(result.reshape(rows_here * lax.axis_size('grp'), feature...  37.7 us
    reduce_scatter x1, waiting for transfers between devices, per_device(): lax.psum_scatter(partial_value.reshape(row_tiles * tile_edge, feature_wid...  21 us
    all_gather x1, blocking collectives, per_device(): block_rows = lax.all_gather(projected, 'rep', axis=0, tiled=True)  15.6 us
    ppermute x4, waiting for transfers between devices, per_device(): earlier.append(lax.ppermute(earlier[-1], 'grp', up))  10.5 us
    ppermute x3, starting transfers between devices, per_device(): later.append(lax.ppermute(later[-1], 'grp', down))  7.93 us
    scatter-add x4, other arithmetic, per_device(): partial_value = partial_value.at[target[:, slot]].add(product)  7.56 us
  transfers between devices with their start and end apart: 10, of which 8 were waited for; matrix products, arithmetic and copies ran while one was open for 0% of the time, Pallas kernels for 0%

profile of v1, /device:TPU:0, one launch (start us, length us, event | category | flops | bytes accessed | tf_op | source)
XLA Modules:
  0.0 265.6 jit_solution(17707081738039124069)
XLA Ops:
  7.2 0.0 copy-start
  7.2 0.0 reduce-scatter.3.cloned.1.call-start
  7.2 0.7 broadcast_select_fusion
  7.9 0.7 broadcast_compare_fusion
  8.6 0.7 convert_rsqrt_fusion
  9.3 0.0 copy-done
  9.3 1.1 fusion.5
  10.4 15.6 %all_gather.3 = bf16[512,256]{1,0:T(8,128)(2,1)S(1)} all-gather(bf16[128,256]{1,0:T(8,128)(2,1)S(1)} %fusion.5), channel_id=1, replica_groups=mesh['grp'=8,'rep'=4] {'rep'}, dimensions={0}, use_global_device_ids=true | all-gather | bytes 327680 | tf_op jit(solution)/shard_map/all_gather | solution.py:58
  26.0 0.1 copy.23
  26.1 0.1 reshape.27
  26.2 0.1 copy.21
  26.3 0.7 copy.22
  26.9 0.0 copy-start.1
  26.9 0.7 gather_fusion
  27.6 0.5 copy-done.1
  28.1 0.0 copy-start.4
  28.1 2.3 fusion
  30.5 0.0 reduce-scatter.3.cloned.1.call-update
  30.5 0.0 reduce-scatter.5.cloned.1.call-start
  30.6 37.7 %reduce-scatter.3.cloned.1.call-done = f32[128,256]{1,0:T(8,128)} async-done(((f32[1024,256]{1,0:T(8,128)}), f32[128,256]{1,0:T(8,128)}) %reduce-scatter.3.cloned.1.call-update) | async-done | bytes 131088 | tf_op jit(solution)/shard_map/reduce_scatter | solution.py:64
  68.2 0.0 copy-done.4
  68.2 1.6 multiply_convert_fusion.1
  69.9 0.0 collective-permute-start
  69.9 4.6 %collective-permute-done = bf16[128,256]{1,0:T(8,128)(2,1)S(1)} collective-permute-done((bf16[128,256]{1,0:T(8,128)(2,1)S(1)}, bf16[128,256]{1,0:T(8,128)(2,1)S(1)}, u32[]{:S(2)}, u32[]{:S(2)}) %collective-permute-start) | collective-permute-done | bytes 65568 | tf_op jit(solution)/shard_map/ppermute | solution.py:28
  74.5 0.0 collective-permute-start.1
  74.5 2.6 collective-permute-start.4
  77.1 2.6 collective-permute-done.1
  79.7 0.0 collective-permute-start.2
  79.7 0.0 collective-permute-done.4
  79.7 2.6 collective-permute-start.5
  82.4 2.0 collective-permute-done.2
  84.3 0.0 collective-permute-start.3
  84.3 0.6 fusion.21
  84.9 0.0 collective-permute-done.5
  84.9 2.6 collective-permute-start.6
  87.6 1.4 collective-permute-done.3
  89.0 0.5 collective-permute-done.6
  89.6 1.4 convolution_bitcast_fusion.3
  91.0 0.3 convolution_bitcast_fusion.2
  91.4 0.3 convolution_bitcast_fusion.1
  91.7 1.3 convolution_bitcast_fusion
  93.0 2.5 copy.27
  95.6 1.4 copy.30
  96.9 0.3 copy.33
  97.3 0.3 copy.36
  97.6 0.0 copy-start.5
  97.7 0.0 copy-done.6
  97.7 2.5 scatter_fusion
  100.2 0.0 copy-done.5
  100.2 2.5 scatter_fusion.1
  102.6 1.3 scatter_fusion.2
  104.0 0.0 copy-start.2
  104.0 0.0 copy-start.3
  104.0 1.3 scatter_fusion.3
  105.3 0.7 slice.61
  106.1 0.0 reduce-scatter.5.cloned.1.call-update
  106.1 0.0 all-reduce.2.cloned.1.call-start
  106.1 21.0 %reduce-scatter.5.cloned.1.call-done = bf16[128,256]{1,0:T(8,128)(2,1)} async-done(((bf16[512,256]{1,0:T(8,128)(2,1)}), bf16[128,256]{1,0:T(8,128)(2,1)}) %reduce-scatter.5.cloned.1.call-update) | async-done | bytes 65552 | tf_op jit(solution)/shard_map/reduce_scatter | solution.py:42
  127.1 0.0 copy-done.2
  127.1 0.0 copy-done.3
  127.1 1.8 fusion.16
  129.0 0.0 all-reduce.2.cloned.1.call-update
  129.0 128.4 %all-reduce.2.cloned.1.call-done = f32[256,256]{1,0:T(8,128)} async-done(((f32[256,256]{1,0:T(8,128)}), f32[256,256]{1,0:T(8,128)}) %all-reduce.2.cloned.1.call-update) | async-done | bytes 262160 | tf_op jit(solution)/shard_map/psum | solution.py:72
  257.4 1.7 copy.67
  (20 shorter events, 0.2 us)
Async XLA Ops:
  7.2 2.1 copy-start
  7.2 61.1 %reduce-scatter.3.cloned.1.call-start = ((), (), s32[]{:S(2)}) async-start(), calls=%async_computation.2 | async-start | bytes 1179648 | tf_op jit(solution)/shard_map/reduce_scatter | solution.py:64
  26.9 1.2 copy-start.1
  28.1 40.1 %copy-start.4 = (bf16[128,256]{1,0:T(8,128)(2,1)S(1)}, bf16[128,256]{1,0:T(8,128)(2,1)}, u32[]{:S(2)}) copy-start(bf16[128,256]{1,0:T(8,128)(2,1)} %param.7) | copy-start | bytes 196612
  30.5 96.6 %reduce-scatter.5.cloned.1.call-start = ((), (), s32[]{:S(2)}) async-start(), calls=%async_computation.3 | async-start | bytes 327680 | tf_op jit(solution)/shard_map/reduce_scatter | solution.py:42
  69.9 4.6 %collective-permute-start = (bf16[128,256]{1,0:T(8,128)(2,1)S(1)}, bf16[128,256]{1,0:T(8,128)(2,1)S(1)}, u32[]{:S(2)}, u32[]{:S(2)}) collective-permute-start(bf16[128,256]{1,0:T(8,128)(2,1)S(1)} %get-tuple-element.10), channel_id=1, source_target_pairs={{0,4},{4,8},{8,12},{12,16},{16,20},{20,24},{24,28},{28,0},{1,5},{5... | collective-permute-start | bytes 196616 | tf_op jit(solution)/shard_map/ppermute | solution.py:28
  74.5 5.2 %collective-permute-start.1 = (bf16[128,256]{1,0:T(8,128)(2,1)S(1)}, bf16[128,256]{1,0:T(8,128)(2,1)S(1)}, u32[]{:S(2)}, u32[]{:S(2)}) collective-permute-start(bf16[128,256]{1,0:T(8,128)(2,1)S(1)} %collective-permute-done), channel_id=1, source_target_pairs={{0,4},{4,8},{8,12},{12,16},{16,20},{20,24},{24,28},{28,0},{1,5},{5... | collective-permute-start | bytes 196616 | tf_op jit(solution)/shard_map/ppermute | solution.py:28
  74.5 5.2 %collective-permute-start.4 = (bf16[128,256]{1,0:T(8,128)(2,1)S(1)}, bf16[128,256]{1,0:T(8,128)(2,1)S(1)}, u32[]{:S(2)}, u32[]{:S(2)}) collective-permute-start(bf16[128,256]{1,0:T(8,128)(2,1)S(1)} %get-tuple-element.10), channel_id=1, source_target_pairs={{0,28},{4,0},{8,4},{12,8},{16,12},{20,16},{24,20},{28,24},{1,29},{... | collective-permute-start | bytes 196616 | tf_op jit(solution)/shard_map/ppermute | solution.py:30
  79.7 4.6 %collective-permute-start.2 = (bf16[128,256]{1,0:T(8,128)(2,1)S(1)}, bf16[128,256]{1,0:T(8,128)(2,1)S(1)}, u32[]{:S(2)}, u32[]{:S(2)}) collective-permute-start(bf16[128,256]{1,0:T(8,128)(2,1)S(1)} %collective-permute-done.1), channel_id=1, source_target_pairs={{0,4},{4,8},{8,12},{12,16},{16,20},{20,24},{24,28},{28,0},{1,5},{5... | collective-permute-start | bytes 196616 | tf_op jit(solution)/shard_map/ppermute | solution.py:28
  79.7 5.2 %collective-permute-start.5 = (bf16[128,256]{1,0:T(8,128)(2,1)S(1)}, bf16[128,256]{1,0:T(8,128)(2,1)S(1)}, u32[]{:S(2)}, u32[]{:S(2)}) collective-permute-start(bf16[128,256]{1,0:T(8,128)(2,1)S(1)} %collective-permute-done.4), channel_id=1, source_target_pairs={{0,28},{4,0},{8,4},{12,8},{16,12},{20,16},{24,20},{28,24},{1,29},{... | collective-permute-start | bytes 196616 | tf_op jit(solution)/shard_map/ppermute | solution.py:30
  84.3 4.6 %collective-permute-start.3 = (bf16[128,256]{1,0:T(8,128)(2,1)S(1)}, bf16[128,256]{1,0:T(8,128)(2,1)S(1)}, u32[]{:S(2)}, u32[]{:S(2)}) collective-permute-start(bf16[128,256]{1,0:T(8,128)(2,1)S(1)} %collective-permute-done.2), channel_id=1, source_target_pairs={{0,4},{4,8},{8,12},{12,16},{16,20},{20,24},{24,28},{28,0},{1,5},{5... | collective-permute-start | bytes 196616 | tf_op jit(solution)/shard_map/ppermute | solution.py:28
  84.9 4.5 %collective-permute-start.6 = (bf16[128,256]{1,0:T(8,128)(2,1)S(1)}, bf16[128,256]{1,0:T(8,128)(2,1)S(1)}, u32[]{:S(2)}, u32[]{:S(2)}) collective-permute-start(bf16[128,256]{1,0:T(8,128)(2,1)S(1)} %collective-permute-done.5), channel_id=1, source_target_pairs={{0,28},{4,0},{8,4},{12,8},{16,12},{20,16},{24,20},{28,24},{1,29},{... | collective-permute-start | bytes 196616 | tf_op jit(solution)/shard_map/ppermute | solution.py:30
  96.9 0.8 copy-start.6
  97.6 2.5 copy-start.5
  104.0 23.2 %copy-start.2 = (bf16[128,256]{1,0:T(8,128)(2,1)S(1)}, bf16[128,256]{1,0:T(8,128)(2,1)}, u32[]{:S(2)}) copy-start(bf16[128,256]{1,0:T(8,128)(2,1)} %param.10) | copy-start | bytes 196612
  104.0 23.2 %copy-start.3 = (bf16[128,256]{1,0:T(8,128)(2,1)S(1)}, bf16[128,256]{1,0:T(8,128)(2,1)}, u32[]{:S(2)}) copy-start(bf16[128,256]{1,0:T(8,128)(2,1)} %param.9) | copy-start | bytes 196612
  106.1 151.3 %all-reduce.2.cloned.1.call-start = ((), (), s32[]{:S(2)}) async-start(), calls=%async_computation.4 | async-start | bytes 524288 | tf_op jit(solution)/shard_map/psum | solution.py:72
Sparse Core Ops, SparseCore 0:
  30.6 37.5 reduce-scatter.2
  106.2 20.8 reduce-scatter.4
  134.1 123.2 all-reduce.1
